TPU v7x, 128 devices: a whole 4x4x4 slice. The times are simulated.
128 devices in a mesh: section: 2 (over core), seq: 64 (over z, x, y).
Axes of the slice: x: 4, y: 4, z: 4, core: 2. Of those that a mesh axis runs over, the one named last changes fastest.
Arguments:
- patches: bfloat16 [32768, 1408], P('seq'), may hold values from -42 to 42
- image_grid: int32 [256, 2], P('seq'), may hold values from 2 to 52, as said below
- image_offsets: int32 [256], P('seq'), may hold values from 0 to 32736, as said below
- dest_positions: int32 [8192], replicated, may hold values from 0 to 16383, as said below
- text_embeds: bfloat16 [256, 64, 1408], P(None, 'seq'), may hold values from -42 to 42
- segment_ids: int32 [256, 64], replicated, may hold values from 0 to 3, as said below
- vision_qkv: bfloat16 [1408, 3, 1408], P(None, None, 'section'), may hold values from -0.15625 to 0.15625
- vision_out: bfloat16 [1408, 1408], P('section'), may hold values from -0.875 to 0.875
- projector: bfloat16 [4, 1408, 1408], P('section'), may hold values from -0.078125 to 0.078125
- decoder_q: bfloat16 [1408, 1408], P(None, 'section'), may hold values from -0.15625 to 0.15625
- decoder_kv: bfloat16 [1408, 2, 176], P(None, None, 'section'), may hold values from -0.15625 to 0.15625
- decoder_out: bfloat16 [1408, 1408], P('section'), may hold values from -0.875 to 0.875
Outputs:
- decoded: bfloat16 [256, 64, 1408], P(None, 'seq')
Inputs may be any that keep to these rules, and one draw needn't show every extreme that they name: `image_grid`: patch rows and columns are even, columns are 8 or 16; the images of one index of seq lie back to back and cover exactly its 512 patches. `image_offsets`: each image's first patch; images are in order, back to back, the first of an index of seq at its first patch. `dest_positions`: the 128 merged rows of one index of seq go, in order, to 128 consecutive prompt positions; the ranges of different indices do not meet. `segment_ids`: never falls along prompt positions; every document number is used.
All inputs are finite; a program needn't handle non-finite values.
Results may differ from a plain program's by a relative error of at most 0.025.
Values may be sent and summed in bfloat16 or wider, within the bound.
No kernel may reach another device: no remote copies, remote signals or barrier semaphores. Data moves between devices by JAX's collectives and lax.ppermute only.
A program may use at most 128 MiB of HBM per device.

v0:
```python
import math
import jax
import jax.numpy as jnp
from jax import lax
from jax.sharding import PartitionSpec as P

D = 1408
HEAD = 88


def layer_norm(values):
    values = values.astype(jnp.float32)
    centred = values - jnp.mean(values, -1, keepdims=True)
    return centred * lax.rsqrt(jnp.mean(centred * centred, -1, keepdims=True) + 1e-06)


def root_norm(values):
    values = values.astype(jnp.float32)
    return values * lax.rsqrt(jnp.mean(values * values, -1, keepdims=True) + 1e-06)


def merge_rows(grid, offsets, count):
    heights = grid[:, 0]
    widths = grid[:, 1]
    group_start = offsets // 4
    group_count = heights * widths // 4
    merged_ids = jnp.arange(count, dtype=jnp.int32)
    inside = (
        (merged_ids[:, None] >= group_start[None, :])
        & (merged_ids[:, None] < (group_start + group_count)[None, :])
    ).astype(jnp.int32)
    first_group = jnp.sum(inside * group_start[None, :], 1)
    first_patch = jnp.sum(inside * offsets[None, :], 1)
    row_width = jnp.sum(inside * widths[None, :], 1)
    within = merged_ids - first_group
    groups_across = row_width // 2
    group_row = within // groups_across
    group_col = within % groups_across
    corner = first_patch + 2 * group_row * row_width + 2 * group_col
    return jnp.stack([corner, corner + 1, corner + row_width, corner + row_width + 1], 1)


def body(
    patches,
    image_grid,
    image_offsets,
    dest_positions,
    text_embeds,
    segment_ids,
    vision_qkv,
    vision_out,
    projector,
    decoder_q,
    decoder_kv,
    decoder_out,
):
    section_index = lax.axis_index("section")
    seq_index = lax.axis_index("seq")
    seq_count = lax.axis_size("seq")
    scale = 3.0 / math.sqrt(HEAD)
    patch_count = patches.shape[0]
    local_heads = vision_out.shape[0] // HEAD
    merged_count = patch_count // 4
    normed = layer_norm(patches).astype(jnp.bfloat16)
    mixed = jnp.dot(normed, vision_qkv.reshape(D, -1), preferred_element_type=jnp.float32).reshape(
        patch_count, 3, local_heads, HEAD
    )
    queries = root_norm(mixed[:, 0]).astype(jnp.bfloat16)
    keys = root_norm(mixed[:, 1]).astype(jnp.bfloat16)
    values = mixed[:, 2].astype(jnp.bfloat16)
    offsets = image_offsets - seq_index * patch_count
    image_of = jnp.sum(
        (jnp.arange(patch_count, dtype=jnp.int32)[:, None] >= offsets[None, :]).astype(jnp.int32), 1
    )
    query_block = math.gcd(patch_count, 512)

    def vision_block(first):
        scores = (
            jnp.einsum("qhd,khd->hqk", queries, keys, preferred_element_type=jnp.float32) * scale
        )
        same = (image_of[:, None] == image_of[None, :])[None]
        weights = jnp.where(same, jnp.exp(scores), jnp.zeros_like(scores))
        totals = jnp.sum(weights, -1)
        mixed_values = jnp.einsum(
            "hqk,khd->qhd", weights.astype(jnp.bfloat16), values, preferred_element_type=jnp.float32
        )
        return (
            (mixed_values / jnp.transpose(totals)[:, :, None])
            .astype(jnp.bfloat16)
            .reshape(query_block, local_heads * HEAD)
        )

    attended = lax.map(
        vision_block, jnp.arange(patch_count // query_block, dtype=jnp.int32) * query_block
    )
    attended = attended.reshape(patch_count, local_heads * HEAD)
    picks = merge_rows(image_grid, offsets, merged_count)
    own_picks = lax.dynamic_slice_in_dim(picks, 2 * section_index, 2, 1).reshape(-1)
    head_terms = jnp.dot(attended, vision_out, preferred_element_type=jnp.float32)
    vision = (patches.astype(jnp.float32) + lax.psum(head_terms, "section")).astype(jnp.bfloat16)
    kept = vision[own_picks]
    merge_terms = jnp.dot(
        kept.reshape(merged_count, 2 * D),
        projector.reshape(2 * D, D),
        preferred_element_type=jnp.float32,
    )
    per_peer = merged_count // seq_count
    run_starts = dest_positions.reshape(seq_count, merged_count)[:, 0]
    own_start = run_starts[seq_index]
    image_rows = lax.psum(merge_terms, "section").astype(jnp.bfloat16)
    received = lax.all_to_all(
        jnp.roll(image_rows.reshape(per_peer, seq_count, image_rows.shape[1]), own_start, axis=1),
        "seq",
        split_axis=1,
        concat_axis=1,
        tiled=True,
    )
    slot_base = jnp.arange(per_peer, dtype=jnp.int32)[:, None] * seq_count
    landing = (
        run_starts[None, :] + slot_base + (seq_index - run_starts[None, :]) % seq_count
    ) // seq_count
    text_rows = text_embeds.shape[0]
    prompt = text_embeds.reshape(text_rows, D).at[landing.reshape(-1)].set(received.reshape(-1, D))
    text_normed = root_norm(prompt).astype(jnp.bfloat16)
    kv_local = decoder_kv.shape[2] // HEAD
    group = local_heads // kv_local
    text_queries = root_norm(
        jnp.dot(text_normed, decoder_q, preferred_element_type=jnp.float32).reshape(
            text_rows, local_heads, HEAD
        )
    )
    text_queries = text_queries.astype(jnp.bfloat16).reshape(text_rows, kv_local, group, HEAD)
    paired = jnp.dot(
        text_normed, decoder_kv.reshape(D, -1), preferred_element_type=jnp.float32
    ).reshape(text_rows, 2, kv_local, HEAD)
    key_rows = root_norm(paired[:, 0]).astype(jnp.bfloat16)
    value_rows = paired[:, 1].astype(jnp.bfloat16)
    shared = jnp.stack([key_rows, value_rows], 1)[None]
    query_places = jnp.arange(text_rows, dtype=jnp.int32) * seq_count + seq_index
    query_segments = lax.dynamic_slice_in_dim(segment_ids, seq_index, 1, 1)[:, 0]
    start_state = (
        jnp.zeros((text_rows, kv_local, group, HEAD), jnp.float32),
        jnp.zeros((text_rows, kv_local, group), jnp.float32),
    )
    piece = lax.all_gather(shared, "seq", axis=0, tiled=True)
    shards = piece.shape[0]
    stride = math.gcd(shards, 8)
    blocks = shards // stride
    key_segments = jnp.transpose(segment_ids).reshape(blocks, stride * text_rows)
    shard_ids = jnp.arange(shards, dtype=jnp.int32)
    key_places = (
        jnp.arange(text_rows, dtype=jnp.int32)[None, :] * seq_count + shard_ids[:, None]
    ).reshape(blocks, stride * text_rows)
    grouped = piece.reshape(blocks, stride * text_rows, 2, kv_local, HEAD)

    def one_block(state, inputs):
        block_pair, block_places, block_segments = inputs
        scores = (
            jnp.einsum(
                "qkgd,lkd->qkgl", text_queries, block_pair[:, 0], preferred_element_type=jnp.float32
            )
            * scale
        )
        allowed = (block_places[None, :] <= query_places[:, None]) & (
            block_segments[None, :] == query_segments[:, None]
        )
        weights = jnp.where(allowed[:, None, None, :], jnp.exp(scores), jnp.zeros_like(scores))
        totals = state[1] + jnp.sum(weights, -1)
        sums = state[0] + jnp.einsum(
            "qkgl,lkd->qkgd",
            weights.astype(jnp.bfloat16),
            block_pair[:, 1],
            preferred_element_type=jnp.float32,
        )
        return ((sums, totals), None)

    result, unused = lax.scan(one_block, start_state, (grouped, key_places, key_segments))
    sums, totals = result
    attended_text = (
        (sums / totals[..., None]).astype(jnp.bfloat16).reshape(text_rows, local_heads * HEAD)
    )
    output_terms = jnp.dot(attended_text, decoder_out, preferred_element_type=jnp.float32)
    decoded = (prompt.astype(jnp.float32) + lax.psum(output_terms, "section")).astype(jnp.bfloat16)
    return decoded.reshape(text_rows, 1, D)


def solution(mesh):
    placed = (
        P("seq", None),
        P("seq", None),
        P("seq"),
        P(),
        P(None, "seq", None),
        P(),
        P(None, None, "section"),
        P("section", None),
        P("section", None, None),
        P(None, "section"),
        P(None, None, "section"),
        P("section", None),
    )
    return jax.shard_map(
        body, mesh=mesh, in_specs=placed, out_specs=P(None, "seq", None), check_vma=False
    )
```

profile of v0, /device:TPU:1, one launch (start us, length us, event | category | flops | bytes accessed | tf_op | source)
XLA Modules:
  0.0 298.4 jit_solution(1817690820470734248)
XLA Ops:
  7.5 1.7 convert_reduce_fusion
  9.9 6.0 %fusion.37 = f32[512,3,8,88]{0,3,2,1:T(8,128)S(1)} fusion(bf16[3,8,88,1408]{3,2,1,0:T(8,128)(2,1)} %bitcast.211, bf16[512,1408]{1,0:T(8,128)(2,1)S(1)} %copy-done.3, f32[512]{0:T(512)S(1)} %add_rsqrt_fusion.3, f32[512]{0:T(512)S(1)} %broadcast_multiply_fusion), kind=kOutput, calls=%fused_computation.47 | convolution fusion | flops 3047948288 | bytes 11718656 | tf_op jit(solution)/shard_map/dot_general | solution.py:65
  16.4 2.5 fusion.18
  18.9 1.8 divide_convert_fusion
  20.7 3.1 %fusion.66 = f32[512,1408]{1,0:T(8,128)} fusion(bf16[512,704]{0,1:T(8,128)(2,1)S(1)} %bitcast.203, bf16[704,1408]{1,0:T(8,128)(2,1)S(1)} %copy-done), kind=kOutput, calls=%fused_computation.146 | convolution fusion | flops 1015021568 | bytes 5586944 | tf_op jit(solution)/shard_map/dot_general | solution.py:99
  27.0 28.8 %all-reduce.4.cloned.1.call-done = f32[512,1408]{1,0:T(8,128)} async-done(((f32[512,1408]{1,0:T(8,128)}), f32[512,1408]{1,0:T(8,128)}) %all-reduce.4.cloned.1.call-update) | async-done | bytes 2883600 | tf_op jit(solution)/shard_map/psum | solution.py:100
  55.8 2.1 fusion.29
  57.9 1.3 gather_fusion
  59.5 4.5 %fusion.67 = f32[128,1408]{1,0:T(8,128)S(1)} fusion(bf16[128,2816]{1,0:T(8,128)(2,1)S(1)} %reshape.607, bf16[2816,1408]{1,0:T(8,128)(2,1)} %bitcast.193), kind=kOutput, calls=%fused_computation.147 | convolution fusion | flops 1015021568 | bytes 9371648 | tf_op jit(solution)/shard_map/dot_general | solution.py:102
  64.0 5.7 %all-reduce.7 = bf16[128,1408]{1,0:T(8,128)(2,1)S(1)} all-reduce(f32[128,1408]{1,0:T(8,128)S(1)} %fusion.67), channel_id=1, replica_groups=mesh['section'=2,'seq'=64] {'section'}, use_global_device_ids=true, to_apply=%region_10.11 | all-reduce | flops 180224 | bytes 1081344 | tf_op jit(solution)/shard_map/psum | solution.py:110
  70.1 1.7 fusion.51
  71.8 10.1 %all-to-all-start = ((bf16[2,64,1408]{2,0,1:T(2,128)(2,1)}), bf16[2,64,1408]{2,0,1:T(2,128)(2,1)S(1)}, u32[]{:S(2)}, u32[]{:S(2)}) async-start(bf16[2,64,1408]{2,0,1:T(2,128)(2,1)} %fusion.51), calls=%async_computation | async-start | bytes 720896 | tf_op jit(solution)/shard_map/all_to_all | solution.py:111
  82.1 10.5 %all-to-all-done = bf16[2,64,1408]{2,0,1:T(2,128)(2,1)S(1)} async-done(((bf16[2,64,1408]{2,0,1:T(2,128)(2,1)}), bf16[2,64,1408]{2,0,1:T(2,128)(2,1)S(1)}, u32[]{:S(2)}, u32[]{:S(2)}) %all-to-all-start) | async-done | bytes 360480 | tf_op jit(solution)/shard_map/all_to_all | solution.py:111
  92.7 1.6 scatter_fusion
  96.0 2.4 fusion.65
  98.5 76.8 %all-gather.3.cloned.1.call-done = bf16[16384,2,1,88]{0,3,1,2:T(8,128)(2,1)} async-done(((bf16[256,2,1,88]{0,3,1,2:T(8,128)(2,1)}), bf16[16384,2,1,88]{0,3,1,2:T(8,128)(2,1)}) %all-gather.3.cloned.1.call-update) | async-done | bytes 5767184 | tf_op jit(solution)/shard_map/all_gather | solution.py:145
  175.3 6.1 %copy.44 = bf16[1,2,11,8,8,2048]{5,4,2,1,0,3:T(8,128)(2,1)} copy(bf16[1,2,11,8,8,2048]{5,4,3,2,1,0:T(8,128)(2,1)} %bitcast.195) | data formatting | bytes 11534336 | tf_op jit(solution)/shard_map/reshape | solution.py:154
  181.4 76.3 %while.4 = (s32[]{:T(128)}, f32[256,1,8,88]{0,3,2,1:T(8,128)S(1)}, f32[256,1,8]{0,2,1:T(8,128)S(1)}, bf16[8,2048,2,1,88]{1,4,2,3,0:T(8,128)(2,1)}, s32[8,2048]{1...) while((s32[]{:T(128)}, f32[256,1,8,88]{0,3,2,1:T(8,128)S(1)}, ...), condition=%wide.region_17.18_spmd.clone, body=%wide.region_15.17_spmd.clone.sunk | while | flops 1503496704 | bytes 39177352 | solution.py:177
  181.5 1.4 compare_and_fusion.2
  184.1 3.9 %fusion.81 = (f32[256,8]{0,1:T(8,128)S(1)}, f32[2048,256,8]{1,0,2:T(8,128)S(1)}) fusion(pred[256,2048]{0,1:T(8,128)(4,1)S(1)} %compare_and_fusion.2, bf16[256,1,8,88]{0,3,2,1:T(8,128)(2,1)S(1)} %get-tuple-element.285, bf16[2048,2,1,88]{0,3,2,1:T(8,128)(2,1)S(1)} %dynamic-slice_bitcast_fusion.2), kind=kOutput, calls=%fused_computation.4.clone.1 | convolution fusion | flops 750778368 | bytes 18030592 | tf_op jit(solution)/shard_map/while/body/eval_jaxpr/qkgd,lkd->qkgl/dot_general | solution.py:159
  188.0 2.9 fusion.82
  191.0 1.4 compare_and_fusion.2
  193.7 3.9 %fusion.81 = (f32[256,8]{0,1:T(8,128)S(1)}, f32[2048,256,8]{1,0,2:T(8,128)S(1)}) fusion(pred[256,2048]{0,1:T(8,128)(4,1)S(1)} %compare_and_fusion.2, bf16[256,1,8,88]{0,3,2,1:T(8,128)(2,1)S(1)} %get-tuple-element.285, bf16[2048,2,1,88]{0,3,2,1:T(8,128)(2,1)S(1)} %dynamic-slice_bitcast_fusion.2), kind=kOutput, calls=%fused_computation.4.clone.1 | convolution fusion | flops 750778368 | bytes 18030592 | tf_op jit(solution)/shard_map/while/body/eval_jaxpr/qkgd,lkd->qkgl/dot_general | solution.py:159
  197.6 2.9 fusion.82
  200.6 1.4 compare_and_fusion.2
  203.2 3.9 %fusion.81 = (f32[256,8]{0,1:T(8,128)S(1)}, f32[2048,256,8]{1,0,2:T(8,128)S(1)}) fusion(pred[256,2048]{0,1:T(8,128)(4,1)S(1)} %compare_and_fusion.2, bf16[256,1,8,88]{0,3,2,1:T(8,128)(2,1)S(1)} %get-tuple-element.285, bf16[2048,2,1,88]{0,3,2,1:T(8,128)(2,1)S(1)} %dynamic-slice_bitcast_fusion.2), kind=kOutput, calls=%fused_computation.4.clone.1 | convolution fusion | flops 750778368 | bytes 18030592 | tf_op jit(solution)/shard_map/while/body/eval_jaxpr/qkgd,lkd->qkgl/dot_general | solution.py:159
  207.1 2.9 fusion.82
  210.1 1.4 compare_and_fusion.2
  211.6 1.2 dynamic-slice_bitcast_fusion.2
  212.8 3.9 %fusion.81 = (f32[256,8]{0,1:T(8,128)S(1)}, f32[2048,256,8]{1,0,2:T(8,128)S(1)}) fusion(pred[256,2048]{0,1:T(8,128)(4,1)S(1)} %compare_and_fusion.2, bf16[256,1,8,88]{0,3,2,1:T(8,128)(2,1)S(1)} %get-tuple-element.285, bf16[2048,2,1,88]{0,3,2,1:T(8,128)(2,1)S(1)} %dynamic-slice_bitcast_fusion.2), kind=kOutput, calls=%fused_computation.4.clone.1 | convolution fusion | flops 750778368 | bytes 18030592 | tf_op jit(solution)/shard_map/while/body/eval_jaxpr/qkgd,lkd->qkgl/dot_general | solution.py:159
  216.6 2.9 fusion.82
  219.6 1.4 compare_and_fusion.2
  221.1 1.2 dynamic-slice_bitcast_fusion.2
  222.3 3.9 %fusion.81 = (f32[256,8]{0,1:T(8,128)S(1)}, f32[2048,256,8]{1,0,2:T(8,128)S(1)}) fusion(pred[256,2048]{0,1:T(8,128)(4,1)S(1)} %compare_and_fusion.2, bf16[256,1,8,88]{0,3,2,1:T(8,128)(2,1)S(1)} %get-tuple-element.285, bf16[2048,2,1,88]{0,3,2,1:T(8,128)(2,1)S(1)} %dynamic-slice_bitcast_fusion.2), kind=kOutput, calls=%fused_computation.4.clone.1 | convolution fusion | flops 750778368 | bytes 18030592 | tf_op jit(solution)/shard_map/while/body/eval_jaxpr/qkgd,lkd->qkgl/dot_general | solution.py:159
  226.2 2.9 fusion.82
  229.2 1.4 compare_and_fusion.2
  230.7 1.2 dynamic-slice_bitcast_fusion.2
  231.9 3.9 %fusion.81 = (f32[256,8]{0,1:T(8,128)S(1)}, f32[2048,256,8]{1,0,2:T(8,128)S(1)}) fusion(pred[256,2048]{0,1:T(8,128)(4,1)S(1)} %compare_and_fusion.2, bf16[256,1,8,88]{0,3,2,1:T(8,128)(2,1)S(1)} %get-tuple-element.285, bf16[2048,2,1,88]{0,3,2,1:T(8,128)(2,1)S(1)} %dynamic-slice_bitcast_fusion.2), kind=kOutput, calls=%fused_computation.4.clone.1 | convolution fusion | flops 750778368 | bytes 18030592 | tf_op jit(solution)/shard_map/while/body/eval_jaxpr/qkgd,lkd->qkgl/dot_general | solution.py:159
  235.7 2.9 fusion.82
  238.7 1.4 compare_and_fusion.2
  241.4 3.9 %fusion.81 = (f32[256,8]{0,1:T(8,128)S(1)}, f32[2048,256,8]{1,0,2:T(8,128)S(1)}) fusion(pred[256,2048]{0,1:T(8,128)(4,1)S(1)} %compare_and_fusion.2, bf16[256,1,8,88]{0,3,2,1:T(8,128)(2,1)S(1)} %get-tuple-element.285, bf16[2048,2,1,88]{0,3,2,1:T(8,128)(2,1)S(1)} %dynamic-slice_bitcast_fusion.2), kind=kOutput, calls=%fused_computation.4.clone.1 | convolution fusion | flops 750778368 | bytes 18030592 | tf_op jit(solution)/shard_map/while/body/eval_jaxpr/qkgd,lkd->qkgl/dot_general | solution.py:159
  245.3 2.9 fusion.82
  248.3 1.4 compare_and_fusion.2
  251.0 3.9 %fusion.81 = (f32[256,8]{0,1:T(8,128)S(1)}, f32[2048,256,8]{1,0,2:T(8,128)S(1)}) fusion(pred[256,2048]{0,1:T(8,128)(4,1)S(1)} %compare_and_fusion.2, bf16[256,1,8,88]{0,3,2,1:T(8,128)(2,1)S(1)} %get-tuple-element.285, bf16[2048,2,1,88]{0,3,2,1:T(8,128)(2,1)S(1)} %dynamic-slice_bitcast_fusion.2), kind=kOutput, calls=%fused_computation.4.clone.1 | convolution fusion | flops 750778368 | bytes 18030592 | tf_op jit(solution)/shard_map/while/body/eval_jaxpr/qkgd,lkd->qkgl/dot_general | solution.py:159
  254.8 2.9 fusion.82
  257.9 3.6 %fusion.68 = f32[256,1408]{1,0:T(8,128)} fusion(bf16[256,704]{0,1:T(8,128)(2,1)S(1)} %bitcast.200, bf16[704,1408]{1,0:T(8,128)(2,1)} %param.25), kind=kOutput, calls=%fused_computation.148 | convolution fusion | flops 507510784 | bytes 3784704 | tf_op jit(solution)/shard_map/dot_general | solution.py:182
  261.5 28.1 %all-reduce.6.cloned.1.call-done = f32[256,1408]{1,0:T(8,128)} async-done(((f32[256,1408]{1,0:T(8,128)}), f32[256,1408]{1,0:T(8,128)}) %all-reduce.6.cloned.1.call-update) | async-done | bytes 1441808 | tf_op jit(solution)/shard_map/psum | solution.py:183
  289.6 2.3 fusion.46
  (101 shorter events, 12.2 us)
Async XLA Ops:
  6.5 14.2 %copy-start = (bf16[704,1408]{1,0:T(8,128)(2,1)S(1)}, bf16[704,1408]{1,0:T(8,128)(2,1)}, u32[]{:S(2)}) copy-start(bf16[704,1408]{1,0:T(8,128)(2,1)} %param.21) | copy-start | bytes 5947396
  6.5 2.6 copy-start.3
  6.5 49.3 %all-reduce.4.cloned.1.call-start = ((), (), s32[]{:S(2)}) async-start(), calls=%async_computation.1 | async-start | bytes 5767168 | tf_op jit(solution)/shard_map/psum | solution.py:100
  20.7 3.1 %copy-start.5 = (s32[8192]{0:T(1024)S(1)}, s32[8192]{0:T(1024)}, u32[]{:S(2)}) copy-start(s32[8192]{0:T(1024)} %param.17) | copy-start | bytes 98308
  23.8 2.6 copy-start.6
  64.0 28.6 %copy-start.2 = (bf16[256,1,1408]{2,0,1:T(8,128)(2,1)S(1)}, bf16[256,1,1408]{2,0,1:T(8,128)(2,1)}, u32[]{:S(2)}) copy-start(bf16[256,1,1408]{2,0,1:T(8,128)(2,1)} %param.18) | copy-start | bytes 2162692
  71.8 20.8 %all-to-all-start = ((bf16[2,64,1408]{2,0,1:T(2,128)(2,1)}), bf16[2,64,1408]{2,0,1:T(2,128)(2,1)S(1)}, u32[]{:S(2)}, u32[]{:S(2)}) async-start(bf16[2,64,1408]{2,0,1:T(2,128)(2,1)} %fusion.51), calls=%async_computation | async-start | bytes 720896 | tf_op jit(solution)/shard_map/all_to_all | solution.py:111
  81.9 93.4 %all-gather.3.cloned.1.call-start = ((), (), s32[]{:S(2)}) async-start(), calls=%async_computation.3 | async-start | bytes 5857280 | tf_op jit(solution)/shard_map/all_gather | solution.py:145
  92.6 1.8 copy-start.7
  94.2 1.6 copy-start.4
  95.7 193.8 %all-reduce.6.cloned.1.call-start = ((), (), s32[]{:S(2)}) async-start(), calls=%async_computation.2 | async-start | bytes 2883584 | tf_op jit(solution)/shard_map/psum | solution.py:183
  257.9 34.0 %copy-start.1 = (bf16[704,1408]{1,0:T(8,128)(2,1)S(1)}, bf16[704,1408]{1,0:T(8,128)(2,1)}, u32[]{:S(2)}) copy-start(bf16[704,1408]{1,0:T(8,128)(2,1)} %param.21) | copy-start | bytes 5947396
Sparse Core Ops, SparseCore 0:
  23.9 31.8 all-reduce.3
  95.8 79.4 all-gather.2
  261.6 27.8 all-reduce.5
where the time goes:
time: 299 us; the launch traced here: 298 us
  waiting for transfers between devices  144 us (48%)
  matrix products  79 us (26%)
  other arithmetic  23 us (8%)
  local copies, waits for them, and re-layouts  20.3 us (7%)
  between operations  15.5 us (5%)
  starting transfers between devices  10.2 us (3%)
  blocking collectives  5.69 us (2%)
    all_gather x1, waiting for transfers between devices, body(): piece = lax.all_gather(shared, 'seq', axis=0, tiled=True)  76.8 us
    dot_general x8, matrix products, one_block(): jnp.einsum('qkgd,lkd->qkgl', text_queries, block_pair[:, 0], preferred_el...  31.2 us
    psum x1, waiting for transfers between devices, body(): lax.psum(head_terms, 'section')  28.8 us
    psum x1, waiting for transfers between devices, body(): lax.psum(output_terms, 'section')  28.1 us
    dot_general x8, matrix products, one_block(): jnp.einsum('qkgl,lkd->qkgd', weights.astype(jnp.bfloat16), block_pair[:,...  23.4 us
    and x8, other arithmetic, one_block(): (block_places[None, :] <= query_places[:, None]) & (block_segments[None,...  11.6 us
    all_to_all x1, waiting for transfers between devices, body(): lax.all_to_all(jnp.roll(image_rows.reshape(per_peer, seq_count, image_row...  10.5 us
    all_to_all x1, starting transfers between devices, body(): lax.all_to_all(jnp.roll(image_rows.reshape(per_peer, seq_count, image_row...  10.1 us
  transfers between devices with their start and end apart: 4, of which 4 were waited for; matrix products, arithmetic and copies ran while one was open for 1% of the time, Pallas kernels for 0%

commit v1 on v0

--- a/solution.py
+++ b/solution.py
@@ -142,7 +142,9 @@
         jnp.zeros((text_rows, kv_local, group, HEAD), jnp.float32),
         jnp.zeros((text_rows, kv_local, group), jnp.float32),
     )
-    piece = lax.all_gather(shared, "seq", axis=0, tiled=True)
+    piece = jnp.concatenate(
+        lax.all_to_all(jnp.stack([shared] * lax.axis_size("seq")), "seq", 0, 0), axis=0
+    )
     shards = piece.shape[0]
     stride = math.gcd(shards, 8)
     blocks = shards // stride

time: 299 us -> 319 us (1.067)
  local copies, waits for them, and re-layouts: 20.3 us -> 42.5 us
  waiting for transfers between devices: 144 us -> 136 us
  starting transfers between devices: 10.2 us -> 16 us
    all_gather x1 -> x0, waiting for transfers between devices: 76.8 us -> none  [body(): piece = lax.all_gather(shared, 'seq', axis=0, tiled=True)]
    all_to_all x0 -> x1, waiting for transfers between devices: none -> 68.9 us  [body(): lax.all_to_all(jnp.stack([shared] * lax.axis_size('seq')), 'seq', 0, 0)]
    another operation x0 -> x2, local copies, waits for them, and re-layouts: none -> 12.7 us  [the longest x1 9.8 us: body(): grouped = piece.reshape(blocks, stride * text_rows, 2, kv_local, HEAD)]
    unnamed x18 -> x19, local copies, waits for them, and re-layouts: 0.05 us -> 8.32 us
    all_to_all x0 -> x1, local copies, waits for them, and re-layouts: none -> 7.27 us  [body(): lax.all_to_all(jnp.stack([shared] * lax.axis_size('seq')), 'seq', 0, 0)]
    reshape x1 -> x0, local copies, waits for them, and re-layouts: 6.1 us -> none  [body(): grouped = piece.reshape(blocks, stride * text_rows, 2, kv_local, HEAD)]
    all_to_all x0 -> x1, starting transfers between devices: none -> 5.82 us  [body(): lax.all_to_all(jnp.stack([shared] * lax.axis_size('seq')), 'seq', 0, 0)]
where the time goes in v1:
time: 319 us; the launch traced here: 318 us
  waiting for transfers between devices  136 us (43%)
  matrix products  79 us (25%)
  local copies, waits for them, and re-layouts  42.5 us (13%)
  other arithmetic  22.4 us (7%)
  starting transfers between devices  16 us (5%)
  between operations  15.8 us (5%)
  blocking collectives  5.69 us (2%)
    all_to_all x1, waiting for transfers between devices, body(): lax.all_to_all(jnp.stack([shared] * lax.axis_size('seq')), 'seq', 0, 0)  68.9 us
    dot_general x8, matrix products, one_block(): jnp.einsum('qkgd,lkd->qkgl', text_queries, block_pair[:, 0], preferred_el...  31.2 us
    psum x1, waiting for transfers between devices, body(): lax.psum(head_terms, 'section')  28.8 us
    psum x1, waiting for transfers between devices, body(): lax.psum(output_terms, 'section')  27.8 us
    dot_general x8, matrix products, one_block(): jnp.einsum('qkgl,lkd->qkgd', weights.astype(jnp.bfloat16), block_pair[:,...  23.4 us
    and x8, other arithmetic, one_block(): (block_places[None, :] <= query_places[:, None]) & (block_segments[None,...  11.6 us
    all_to_all x1, waiting for transfers between devices, body(): lax.all_to_all(jnp.roll(image_rows.reshape(per_peer, seq_count, image_row...  10.5 us
    all_to_all x1, starting transfers between devices, body(): lax.all_to_all(jnp.roll(image_rows.reshape(per_peer, seq_count, image_row...  10.1 us
  transfers between devices with their start and end apart: 4, of which 4 were waited for; matrix products, arithmetic and copies ran while one was open for 1% of the time, Pallas kernels for 0%

profile of v1, /device:TPU:1, one launch (start us, length us, event | category | flops | bytes accessed | tf_op | source)
XLA Modules:
  0.0 317.9 jit_solution(9741131239717566231)
XLA Ops:
  7.5 1.7 convert_reduce_fusion
  9.9 6.0 %fusion.37 = f32[512,3,8,88]{0,3,2,1:T(8,128)S(1)} fusion(bf16[3,8,88,1408]{3,2,1,0:T(8,128)(2,1)} %bitcast.211, bf16[512,1408]{1,0:T(8,128)(2,1)S(1)} %copy-done.3, f32[512]{0:T(512)S(1)} %add_rsqrt_fusion.3, f32[512]{0:T(512)S(1)} %broadcast_multiply_fusion), kind=kOutput, calls=%fused_computation.46 | convolution fusion | flops 3047948288 | bytes 11718656 | tf_op jit(solution)/shard_map/dot_general | solution.py:65
  16.4 2.5 fusion.18
  18.9 1.8 divide_convert_fusion
  20.7 3.1 fusion.66
  27.0 28.8 %all-reduce.4.cloned.1.call-done = f32[512,1408]{1,0:T(8,128)} async-done(((f32[512,1408]{1,0:T(8,128)}), f32[512,1408]{1,0:T(8,128)}) %all-reduce.4.cloned.1.call-update) | async-done | bytes 2883600 | tf_op jit(solution)/shard_map/psum | solution.py:100
  55.8 2.1 fusion.29
  59.5 4.5 %fusion.67 = f32[128,1408]{1,0:T(8,128)S(1)} fusion(bf16[128,2816]{1,0:T(8,128)(2,1)S(1)} %reshape.607, bf16[2816,1408]{1,0:T(8,128)(2,1)} %bitcast.195), kind=kOutput, calls=%fused_computation.146 | convolution fusion | flops 1015021568 | bytes 9371648 | tf_op jit(solution)/shard_map/dot_general | solution.py:102
  64.0 5.7 %all-reduce.7 = bf16[128,1408]{1,0:T(8,128)(2,1)S(1)} all-reduce(f32[128,1408]{1,0:T(8,128)S(1)} %fusion.67), channel_id=1, replica_groups=mesh['section'=2,'seq'=64] {'section'}, use_global_device_ids=true, to_apply=%region_10.11 | all-reduce | flops 180224 | bytes 1081344 | tf_op jit(solution)/shard_map/psum | solution.py:110
  70.1 1.7 fusion.51
  71.8 10.1 %all-to-all-start = ((bf16[2,64,1408]{2,0,1:T(2,128)(2,1)}), bf16[2,64,1408]{2,0,1:T(2,128)(2,1)S(1)}, u32[]{:S(2)}, u32[]{:S(2)}) async-start(bf16[2,64,1408]{2,0,1:T(2,128)(2,1)} %fusion.51), calls=%async_computation | async-start | bytes 720896 | tf_op jit(solution)/shard_map/all_to_all | solution.py:111
  82.1 10.5 %all-to-all-done = bf16[2,64,1408]{2,0,1:T(2,128)(2,1)S(1)} async-done(((bf16[2,64,1408]{2,0,1:T(2,128)(2,1)}), bf16[2,64,1408]{2,0,1:T(2,128)(2,1)S(1)}, u32[]{:S(2)}, u32[]{:S(2)}) %all-to-all-start) | async-done | bytes 360480 | tf_op jit(solution)/shard_map/all_to_all | solution.py:111
  92.7 1.6 scatter_fusion
  95.1 2.9 stack.20
  98.0 5.8 %all-to-all-start.1 = ((bf16[64,1,256,2,1,88]{2,5,3,4,1,0:T(8,128)(2,1)}), bf16[64,1,256,2,1,88]{2,5,3,4,1,0:T(8,128)(2,1)}, u32[]{:S(2)}, u32[]{:S(2)}) async-start(bf16[64,1,256,2,1,88]{2,5,3,4,1,0:T(8,128)(2,1)} %stack.20), calls=%async_computation.1 | async-start | bytes 11534336 | tf_op jit(solution)/shard_map/all_to_all | solution.py:146
  104.1 2.4 fusion.65
  106.6 68.9 %all-to-all-done.1 = bf16[64,1,256,2,1,88]{2,5,3,4,1,0:T(8,128)(2,1)} async-done(((bf16[64,1,256,2,1,88]{2,5,3,4,1,0:T(8,128)(2,1)}), bf16[64,1,256,2,1,88]{2,5,3,4,1,0:T(8,128)(2,1)}, u32[]{:S(2)}, u32[]{:S(2)}) %all-to-all-start.1) | async-done | bytes 5767200 | tf_op jit(solution)/shard_map/all_to_all | solution.py:146
  175.5 7.3 %copy.38 = bf16[64,1,256,2,1,88]{2,0,5,3,4,1:T(8,128)(2,1)} copy(bf16[64,1,256,2,1,88]{2,5,3,4,1,0:T(8,128)(2,1)} %all-to-all-done.1) | data formatting | bytes 11534336 | tf_op jit(solution)/shard_map/all_to_all | solution.py:146
  182.8 9.8 %reshape_reshape.3 = bf16[8,2048,2,1,88]{1,0,4,2,3:T(8,128)(2,1)} reshape(bf16[64,1,256,2,1,88]{2,0,5,3,4,1:T(8,128)(2,1)} %copy.38) | data formatting | bytes 11534336 | tf_op jit(solution)/shard_map/reshape;reshape | solution.py:156
  192.6 8.3 %copy.39 = bf16[8,2048,2,1,88]{1,4,2,3,0:T(8,128)(2,1)} copy(bf16[8,2048,2,1,88]{1,0,4,2,3:T(8,128)(2,1)} %reshape_reshape.3) | data formatting | bytes 11534336
  200.9 76.3 %while.4 = (s32[]{:T(128)}, f32[256,1,8,88]{0,3,2,1:T(8,128)S(1)}, f32[256,1,8]{0,2,1:T(8,128)S(1)}, bf16[8,2048,2,1,88]{1,4,2,3,0:T(8,128)(2,1)}, s32[8,2048]{1...) while((s32[]{:T(128)}, f32[256,1,8,88]{0,3,2,1:T(8,128)S(1)}, ...), condition=%wide.region_17.18_spmd.clone, body=%wide.region_15.17_spmd.clone.sunk | while | flops 1503496704 | bytes 39177352 | solution.py:179
  200.9 1.4 compare_and_fusion.2
  203.5 3.9 %fusion.81 = (f32[256,8]{0,1:T(8,128)S(1)}, f32[2048,256,8]{1,0,2:T(8,128)S(1)}) fusion(pred[256,2048]{0,1:T(8,128)(4,1)S(1)} %compare_and_fusion.2, bf16[256,1,8,88]{0,3,2,1:T(8,128)(2,1)S(1)} %get-tuple-element.276, bf16[2048,2,1,88]{0,3,2,1:T(8,128)(2,1)S(1)} %dynamic-slice_bitcast_fusion.2), kind=kOutput, calls=%fused_computation.4.clone.1 | convolution fusion | flops 750778368 | bytes 18030592 | tf_op jit(solution)/shard_map/while/body/eval_jaxpr/qkgd,lkd->qkgl/dot_general | solution.py:161
  207.4 2.9 fusion.82
  210.4 1.4 compare_and_fusion.2
  213.1 3.9 %fusion.81 = (f32[256,8]{0,1:T(8,128)S(1)}, f32[2048,256,8]{1,0,2:T(8,128)S(1)}) fusion(pred[256,2048]{0,1:T(8,128)(4,1)S(1)} %compare_and_fusion.2, bf16[256,1,8,88]{0,3,2,1:T(8,128)(2,1)S(1)} %get-tuple-element.276, bf16[2048,2,1,88]{0,3,2,1:T(8,128)(2,1)S(1)} %dynamic-slice_bitcast_fusion.2), kind=kOutput, calls=%fused_computation.4.clone.1 | convolution fusion | flops 750778368 | bytes 18030592 | tf_op jit(solution)/shard_map/while/body/eval_jaxpr/qkgd,lkd->qkgl/dot_general | solution.py:161
  217.0 2.9 fusion.82
  220.0 1.4 compare_and_fusion.2
  222.6 3.9 %fusion.81 = (f32[256,8]{0,1:T(8,128)S(1)}, f32[2048,256,8]{1,0,2:T(8,128)S(1)}) fusion(pred[256,2048]{0,1:T(8,128)(4,1)S(1)} %compare_and_fusion.2, bf16[256,1,8,88]{0,3,2,1:T(8,128)(2,1)S(1)} %get-tuple-element.276, bf16[2048,2,1,88]{0,3,2,1:T(8,128)(2,1)S(1)} %dynamic-slice_bitcast_fusion.2), kind=kOutput, calls=%fused_computation.4.clone.1 | convolution fusion | flops 750778368 | bytes 18030592 | tf_op jit(solution)/shard_map/while/body/eval_jaxpr/qkgd,lkd->qkgl/dot_general | solution.py:161
  226.5 2.9 fusion.82
  229.5 1.4 compare_and_fusion.2
  232.1 3.9 %fusion.81 = (f32[256,8]{0,1:T(8,128)S(1)}, f32[2048,256,8]{1,0,2:T(8,128)S(1)}) fusion(pred[256,2048]{0,1:T(8,128)(4,1)S(1)} %compare_and_fusion.2, bf16[256,1,8,88]{0,3,2,1:T(8,128)(2,1)S(1)} %get-tuple-element.276, bf16[2048,2,1,88]{0,3,2,1:T(8,128)(2,1)S(1)} %dynamic-slice_bitcast_fusion.2), kind=kOutput, calls=%fused_computation.4.clone.1 | convolution fusion | flops 750778368 | bytes 18030592 | tf_op jit(solution)/shard_map/while/body/eval_jaxpr/qkgd,lkd->qkgl/dot_general | solution.py:161
  236.1 2.9 fusion.82
  239.1 1.4 compare_and_fusion.2
  241.7 3.9 %fusion.81 = (f32[256,8]{0,1:T(8,128)S(1)}, f32[2048,256,8]{1,0,2:T(8,128)S(1)}) fusion(pred[256,2048]{0,1:T(8,128)(4,1)S(1)} %compare_and_fusion.2, bf16[256,1,8,88]{0,3,2,1:T(8,128)(2,1)S(1)} %get-tuple-element.276, bf16[2048,2,1,88]{0,3,2,1:T(8,128)(2,1)S(1)} %dynamic-slice_bitcast_fusion.2), kind=kOutput, calls=%fused_computation.4.clone.1 | convolution fusion | flops 750778368 | bytes 18030592 | tf_op jit(solution)/shard_map/while/body/eval_jaxpr/qkgd,lkd->qkgl/dot_general | solution.py:161
  245.6 2.9 fusion.82
  248.6 1.4 compare_and_fusion.2
  251.2 3.9 %fusion.81 = (f32[256,8]{0,1:T(8,128)S(1)}, f32[2048,256,8]{1,0,2:T(8,128)S(1)}) fusion(pred[256,2048]{0,1:T(8,128)(4,1)S(1)} %compare_and_fusion.2, bf16[256,1,8,88]{0,3,2,1:T(8,128)(2,1)S(1)} %get-tuple-element.276, bf16[2048,2,1,88]{0,3,2,1:T(8,128)(2,1)S(1)} %dynamic-slice_bitcast_fusion.2), kind=kOutput, calls=%fused_computation.4.clone.1 | convolution fusion | flops 750778368 | bytes 18030592 | tf_op jit(solution)/shard_map/while/body/eval_jaxpr/qkgd,lkd->qkgl/dot_general | solution.py:161
  255.2 2.9 fusion.82
  258.2 1.4 compare_and_fusion.2
  260.8 3.9 %fusion.81 = (f32[256,8]{0,1:T(8,128)S(1)}, f32[2048,256,8]{1,0,2:T(8,128)S(1)}) fusion(pred[256,2048]{0,1:T(8,128)(4,1)S(1)} %compare_and_fusion.2, bf16[256,1,8,88]{0,3,2,1:T(8,128)(2,1)S(1)} %get-tuple-element.276, bf16[2048,2,1,88]{0,3,2,1:T(8,128)(2,1)S(1)} %dynamic-slice_bitcast_fusion.2), kind=kOutput, calls=%fused_computation.4.clone.1 | convolution fusion | flops 750778368 | bytes 18030592 | tf_op jit(solution)/shard_map/while/body/eval_jaxpr/qkgd,lkd->qkgl/dot_general | solution.py:161
  264.7 2.9 fusion.82
  267.7 1.4 compare_and_fusion.2
  270.3 3.9 %fusion.81 = (f32[256,8]{0,1:T(8,128)S(1)}, f32[2048,256,8]{1,0,2:T(8,128)S(1)}) fusion(pred[256,2048]{0,1:T(8,128)(4,1)S(1)} %compare_and_fusion.2, bf16[256,1,8,88]{0,3,2,1:T(8,128)(2,1)S(1)} %get-tuple-element.276, bf16[2048,2,1,88]{0,3,2,1:T(8,128)(2,1)S(1)} %dynamic-slice_bitcast_fusion.2), kind=kOutput, calls=%fused_computation.4.clone.1 | convolution fusion | flops 750778368 | bytes 18030592 | tf_op jit(solution)/shard_map/while/body/eval_jaxpr/qkgd,lkd->qkgl/dot_general | solution.py:161
  274.3 2.9 fusion.82
  277.3 3.6 %fusion.68 = f32[256,1408]{1,0:T(8,128)} fusion(bf16[256,704]{0,1:T(8,128)(2,1)S(1)} %bitcast.200, bf16[704,1408]{1,0:T(8,128)(2,1)} %param.25), kind=kOutput, calls=%fused_computation.147 | convolution fusion | flops 507510784 | bytes 3784704 | tf_op jit(solution)/shard_map/dot_general | solution.py:184
  280.9 27.8 %all-reduce.6.cloned.1.call-done = f32[256,1408]{1,0:T(8,128)} async-done(((f32[256,1408]{1,0:T(8,128)}), f32[256,1408]{1,0:T(8,128)}) %all-reduce.6.cloned.1.call-update) | async-done | bytes 1441808 | tf_op jit(solution)/shard_map/psum | solution.py:185
  308.7 2.3 fusion.46
  (103 shorter events, 16.3 us)
Async XLA Ops:
  6.5 14.2 %copy-start = (bf16[704,1408]{1,0:T(8,128)(2,1)S(1)}, bf16[704,1408]{1,0:T(8,128)(2,1)}, u32[]{:S(2)}) copy-start(bf16[704,1408]{1,0:T(8,128)(2,1)} %param.21) | copy-start | bytes 5947396
  6.5 2.6 copy-start.3
  6.5 49.3 %all-reduce.4.cloned.1.call-start = ((), (), s32[]{:S(2)}) async-start(), calls=%async_computation.2 | async-start | bytes 5767168 | tf_op jit(solution)/shard_map/psum | solution.py:100
  20.7 3.1 copy-start.5
  23.8 2.6 copy-start.6
  64.0 28.6 %copy-start.2 = (bf16[256,1,1408]{2,0,1:T(8,128)(2,1)S(1)}, bf16[256,1,1408]{2,0,1:T(8,128)(2,1)}, u32[]{:S(2)}) copy-start(bf16[256,1,1408]{2,0,1:T(8,128)(2,1)} %param.18) | copy-start | bytes 2162692
  71.8 20.8 %all-to-all-start = ((bf16[2,64,1408]{2,0,1:T(2,128)(2,1)}), bf16[2,64,1408]{2,0,1:T(2,128)(2,1)S(1)}, u32[]{:S(2)}, u32[]{:S(2)}) async-start(bf16[2,64,1408]{2,0,1:T(2,128)(2,1)} %fusion.51), calls=%async_computation | async-start | bytes 720896 | tf_op jit(solution)/shard_map/all_to_all | solution.py:111
  92.6 1.8 copy-start.7
  98.0 5.9 %copy-start.4 = (s32[256,64]{0,1:T(8,128)S(1)}, s32[256,64]{0,1:T(8,128)}, u32[]{:S(2)}) copy-start(s32[256,64]{0,1:T(8,128)} %param.19) | copy-start | bytes 196612
  98.0 77.6 %all-to-all-start.1 = ((bf16[64,1,256,2,1,88]{2,5,3,4,1,0:T(8,128)(2,1)}), bf16[64,1,256,2,1,88]{2,5,3,4,1,0:T(8,128)(2,1)}, u32[]{:S(2)}, u32[]{:S(2)}) async-start(bf16[64,1,256,2,1,88]{2,5,3,4,1,0:T(8,128)(2,1)} %stack.20), calls=%async_computation.1 | async-start | bytes 11534336 | tf_op jit(solution)/shard_map/all_to_all | solution.py:146
  103.8 204.9 %all-reduce.6.cloned.1.call-start = ((), (), s32[]{:S(2)}) async-start(), calls=%async_computation.3 | async-start | bytes 2883584 | tf_op jit(solution)/shard_map/psum | solution.py:185
  277.3 33.8 %copy-start.1 = (bf16[704,1408]{1,0:T(8,128)(2,1)S(1)}, bf16[704,1408]{1,0:T(8,128)(2,1)}, u32[]{:S(2)}) copy-start(bf16[704,1408]{1,0:T(8,128)(2,1)} %param.21) | copy-start | bytes 5947396
Sparse Core Ops, SparseCore 0:
  23.9 31.8 all-reduce.3
  281.1 27.6 all-reduce.5
